TPU v7x, 256 devices: a whole 4x4x8 slice. The times are simulated.
256 devices in a mesh: shot: 16 (over y, x_lo, core), space: 16 (over z, x_hi).
Axes of the slice: x: 4 (x_hi: 2, x_lo: 2; x = x_hi * 2 + x_lo), y: 4, z: 8, core: 2. Of those that a mesh axis runs over, the one named last changes fastest.
Arguments:
- courant: float32 [128, 128, 128], P('space'), may hold values from 0.03 to 0.18
- checkpoint: float32 [16, 2, 2048, 8, 128], P('shot', None, 'space'), may hold values from -6 to 6
- block_target: int32 [16, 2048], P('shot'), may hold values from 0 to 2047, as said below
- adjoint_state: float32 [16, 2, 128, 128, 128], P('shot', None, 'space'), may hold values from -6 to 6
- wavelet: float32 [16, 4], P('shot'), may hold values from -8 to 8
- source_cell: int32 [16], P('shot'), may hold values from 0 to 2097151
- receiver_cell: int32 [16, 512], P('shot'), may hold values from 0 to 2097151
- residual: float32 [16, 4, 512], P('shot'), may hold values from -6 to 6
- check_rows: int32 [16, 128, 16], P('space'), may hold values from 0 to 1023
Outputs:
- gradient: float32 [128, 128, 128], P('space', 'shot')
- adjoint_carry: float32 [16, 2, 128, 128, 128], P('shot', None, 'space')
- checksums: float32 [16, 128, 128], P('space', 'shot')
Inputs may be any that keep to these rules, and one draw needn't show every extreme that they name: `block_target`: each shot's row is a permutation of the block positions. The stored blocks of one device (aligned blocks of 128 entries) name at most 32 positions of any one slab (128 consecutive positions); each device names exactly 32 of one slab, and each slab is named exactly 32 times by one device.
All inputs are finite; a program needn't handle non-finite values.
Results may differ from a plain program's by a relative error of at most 0.0003.
Values sent between devices are 32-bit elements; how exact they have to be, the bound alone decides.
No kernel may reach another device: no remote copies, remote signals or barrier semaphores. Data moves between devices by JAX's collectives and lax.ppermute only.
A program may use at most 128 MiB of HBM per device.

v0:
```python
import jax
import jax.numpy as jnp
from jax import lax
from jax.sharding import PartitionSpec as P

STENCIL = (-205.0 / 72.0, 8.0 / 5.0, -1.0 / 5.0, 8.0 / 315.0, -1.0 / 560.0)


def padded_2(array, sides, width):
    for axis, dim in sides:
        devices, length = (lax.axis_size(axis), array.shape[dim])
        up = [(i, (i + 1) % devices) for i in range(devices - 1)]
        down = [(j, i) for i, j in up]
        last = lax.slice_in_dim(array, length - width, length, axis=dim)
        initial = lax.slice_in_dim(array, 0, width, axis=dim)
        before = lax.ppermute(last, axis, up)
        after = lax.ppermute(initial, axis, down)
        array = jnp.concatenate([before, array, after], axis=dim)
    return array


def laplace(field):
    length = field.shape[0] - 8
    height = field.shape[1]
    breadth = field.shape[2]
    padded = jnp.pad(field, ((0, 0), (4, 4), (4, 4)))
    summed = 3.0 * STENCIL[0] * padded[4 : 4 + length, 4 : 4 + height, 4 : 4 + breadth]
    for offset in range(1, 5):
        summed = summed + STENCIL[offset] * (
            padded[4 + offset : 4 + offset + length, 4 : 4 + height, 4 : 4 + breadth]
            + padded[4 - offset : 4 - offset + length, 4 : 4 + height, 4 : 4 + breadth]
        )
    for offset in range(1, 5):
        summed = summed + STENCIL[offset] * (
            padded[4 : 4 + length, 4 + offset : 4 + offset + height, 4 : 4 + breadth]
            + padded[4 : 4 + length, 4 - offset : 4 - offset + height, 4 : 4 + breadth]
        )
    for offset in range(1, 5):
        summed = summed + STENCIL[offset] * (
            padded[4 : 4 + length, 4 : 4 + height, 4 + offset : 4 + offset + breadth]
            + padded[4 : 4 + length, 4 : 4 + height, 4 - offset : 4 - offset + breadth]
        )
    return summed


def inject(field, cell_index, values, first_row):
    plane_cells = field.shape[1] * field.shape[2]
    local_cell = cell_index - first_row * plane_cells
    inside = (local_cell >= 0) & (local_cell < field.shape[0] * plane_cells)
    target = jnp.where(inside, local_cell, field.shape[0] * plane_cells)
    flattened = field.reshape(-1).at[target].add(values, mode="drop")
    return flattened.reshape(field.shape)


def advance(before, current_ext, courant, wave_value, source, first_row):
    following = 2.0 * current_ext[4:-4] - before + courant * laplace(current_ext)
    return inject(following, source, wave_value, first_row)


def retreat(following, current, weighted_ext, values, cell_index, first_row):
    earlier = 2.0 * current - following + laplace(weighted_ext)
    return inject(earlier, cell_index, values, first_row)


def extend(field):
    return padded_2(field, (("space", 0),), 4)


def body(
    courant,
    checkpoint,
    block_target,
    adjoint_state,
    wavelet,
    source_cell,
    receiver_cell,
    residual,
    check_rows,
):
    devices = lax.axis_size("space")
    position = lax.axis_index("space")
    length, height, breadth = courant.shape
    first_row = position * length
    per_device = checkpoint.shape[2]
    block_rows = checkpoint.shape[3]
    capacity = per_device // 4
    targets = block_target[0]
    payload = checkpoint[0]
    peers = targets // per_device
    matches = (peers[:, None] == jnp.arange(devices, dtype=jnp.int32)[None, :]).astype(jnp.int32)
    grouped = matches.reshape(devices, per_device, devices)
    ranking = jnp.sum((jnp.cumsum(grouped, axis=1) - grouped) * grouped, axis=2)
    peer_grid = peers.reshape(devices, per_device)
    own_peers = lax.dynamic_index_in_dim(peer_grid, position, 0, keepdims=False)
    own_ranks = lax.dynamic_index_in_dim(ranking, position, 0, keepdims=False)
    slot_of = own_peers * capacity + own_ranks
    outgoing = (
        jnp.zeros((2, devices * capacity, block_rows, breadth), jnp.float32)
        .at[:, slot_of]
        .set(payload)
    )
    outgoing = outgoing.reshape(2, devices, capacity, block_rows, breadth)
    incoming = lax.all_to_all(outgoing, "space", split_axis=1, concat_axis=1, tiled=True)
    incoming = incoming.reshape(2, devices * capacity, block_rows, breadth)
    sender_grid = jnp.arange(devices, dtype=jnp.int32)[:, None] * capacity + ranking
    owned = peer_grid == position
    local_block = (targets % per_device).reshape(devices, per_device)
    where_from = (
        jnp.zeros((per_device,), jnp.int32)
        .at[jnp.where(owned, local_block, per_device).reshape(-1)]
        .set(sender_grid.reshape(-1), mode="drop")
    )
    placed = jnp.take(incoming, where_from, axis=1)
    levels = placed.reshape(2, length, height, breadth)
    wavelet_row = wavelet[0]
    receivers = receiver_cell[0]
    traces = residual[0]
    horizon = wavelet_row.shape[0]
    fields = [levels[0], levels[1]]
    adjoints = [None] * (horizon + 2)
    adjoints[horizon + 1] = adjoint_state[0, 0]
    adjoints[horizon] = adjoint_state[0, 1]
    for moment in range(1, horizon + 1):
        fields.append(
            advance(
                fields[-2],
                extend(fields[-1]),
                courant,
                wavelet_row[moment - 1 : moment],
                source_cell,
                first_row,
            )
        )
    for moment in range(horizon, 0, -1):
        weighted = extend(courant * adjoints[moment])
        adjoints[moment - 1] = retreat(
            adjoints[moment + 1],
            adjoints[moment],
            weighted,
            traces[moment - 1],
            receivers,
            first_row,
        )
    partial_value = jnp.zeros((length, height, breadth), jnp.float32)
    for moment in range(1, horizon + 1):
        partial_value = partial_value + adjoints[moment] * (
            fields[moment + 1] - 2.0 * fields[moment] + fields[moment - 1]
        )
    slab_rows = partial_value.reshape(length * height, breadth)
    check_part = jnp.sum(slab_rows[check_rows[0]], axis=1)
    grad_share = lax.psum_scatter(partial_value, "shot", scatter_dimension=1, tiled=True)
    check_share = lax.psum_scatter(check_part, "shot", scatter_dimension=0, tiled=True)
    adjoint_carry = jnp.stack([adjoints[1], adjoints[0]])[None]
    return (grad_share, adjoint_carry, check_share[None])


def solution(mesh):
    in_specs = (
        P("space", None, None),
        P("shot", None, "space", None, None),
        P("shot", None),
        P("shot", None, "space", None, None),
        P("shot", None),
        P("shot"),
        P("shot", None),
        P("shot", None, None),
        P("space", None, None),
    )
    out_specs = (
        P("space", "shot", None),
        P("shot", None, "space", None, None),
        P("space", "shot", None),
    )
    return jax.shard_map(body, mesh=mesh, in_specs=in_specs, out_specs=out_specs, check_vma=False)
```

profile of v0, /device:TPU:4, one launch (start us, length us, event | category | flops | bytes accessed | tf_op | source)
XLA Modules:
  0.0 528.2 jit_solution(15008843376083713308)
XLA Ops:
  14.6 13.6 %scatter_fusion.3 = f32[2,512,8,128]{3,2,1,0:T(8,128)} fusion(f32[2,512,8,128]{3,2,1,0:T(8,128)} %broadcast_in_dim.48, s32[128]{0:T(128)S(1)} %fusion.310, f32[128,2,8,128]{3,2,1,0:T(8,128)S(1)} %copy.34), kind=kCustom, calls=%fused_computation.6 | custom fusion | bytes 3146240 | tf_op jit(solution)/shard_map/scatter | solution.py:100
  28.2 4.7 copy.35
  32.9 11.6 %all-to-all-start = ((f32[2,16,32,8,128]{4,3,2,0,1:T(8,128)}), f32[2,16,32,8,128]{4,3,2,0,1:T(8,128)}, u32[]{:S(2)}, u32[]{:S(2)}) async-start(f32[2,16,32,8,128]{4,3,2,0,1:T(8,128)} %copy.35), calls=%async_computation | async-start | bytes 8388608 | tf_op jit(solution)/shard_map/all_to_all | solution.py:103
  46.7 6.2 %collective-permute-start.1 = (f32[4,128,128]{2,1,0:T(8,128)S(1)}, f32[4,128,128]{2,1,0:T(8,128)S(1)}, u32[]{:S(2)}, u32[]{:S(2)}) collective-permute-start(f32[4,128,128]{2,1,0:T(8,128)S(1)} %get-tuple-element.64), channel_id=1, source_target_pairs={{0,1},{1,2},{2,3},{3,4},{4,5},{5,6},{6,7},{7,8},{8,9},{9,10},{10,1... | collective-permute-start | bytes 786440 | tf_op jit(solution)/shard_map/ppermute | solution.py:16
  53.2 8.0 %scatter_custom_fusion.3 = s32[128]{0:T(128)S(1)} fusion(s32[2048]{0:T(1024)S(1)} %bitcast.210, s32[2048]{0:T(1024)S(1)} %add_bitcast_fusion, s32[]{:T(128)} %constant.152.clone.1), kind=kCustom, calls=%fused_computation.564 | custom fusion | bytes 516 | tf_op jit(solution)/shard_map/scatter | solution.py:111
  63.5 82.6 %collective-permute-done = f32[4,128,128]{2,1,0:T(8,128)S(1)} collective-permute-done((f32[4,128,128]{2,1,0:T(8,128)S(1)}, f32[4,128,128]{2,1,0:T(8,128)S(1)}, u32[]{:S(2)}, u32[]{:S(2)}) %collective-permute-start) | collective-permute-done | bytes 262176 | tf_op jit(solution)/shard_map/ppermute | solution.py:17
  148.6 3.5 fusion.199
  152.1 3.7 scatter_fusion
  158.0 6.3 %collective-permute-start.3 = (f32[4,128,128]{2,1,0:T(8,128)S(1)}, f32[4,128,128]{2,1,0:T(8,128)}, u32[]{:S(2)}, u32[]{:S(2)}) collective-permute-start(f32[4,128,128]{2,1,0:T(8,128)S(1)} %get-tuple-element.62), channel_id=1, source_target_pairs={{0,1},{1,2},{2,3},{3,4},{4,5},{5,6},{6,7},{7,8},{8,9},{9,10},{10,1... | collective-permute-start | bytes 786440 | tf_op jit(solution)/shard_map/ppermute | solution.py:16
  167.7 5.6 %collective-permute-done.3 = f32[4,128,128]{2,1,0:T(8,128)} collective-permute-done((f32[4,128,128]{2,1,0:T(8,128)S(1)}, f32[4,128,128]{2,1,0:T(8,128)}, u32[]{:S(2)}, u32[]{:S(2)}) %collective-permute-start.3) | collective-permute-done | bytes 262176 | tf_op jit(solution)/shard_map/ppermute | solution.py:16
  175.1 4.7 copy.36
  179.8 4.0 gather_fusion
  187.2 6.6 %collective-permute-start.7 = (f32[4,128,128]{2,1,0:T(8,128)S(1)}, f32[4,128,128]{2,1,0:T(8,128)S(1)}, u32[]{:S(2)}, u32[]{:S(2)}) collective-permute-start(f32[4,128,128]{2,1,0:T(8,128)S(1)} %bitcast.199), channel_id=1, source_target_pairs={{0,1},{1,2},{2,3},{3,4},{4,5},{5,6},{6,7},{7,8},{8,9},{9,10},{10,1... | collective-permute-start | bytes 786440 | tf_op jit(solution)/shard_map/ppermute | solution.py:16
  197.9 5.5 %collective-permute-done.7 = f32[4,128,128]{2,1,0:T(8,128)S(1)} collective-permute-done((f32[4,128,128]{2,1,0:T(8,128)S(1)}, f32[4,128,128]{2,1,0:T(8,128)S(1)}, u32[]{:S(2)}, u32[]{:S(2)}) %collective-permute-start.7) | collective-permute-done | bytes 262176 | tf_op jit(solution)/shard_map/ppermute | solution.py:16
  205.4 11.8 %fusion.124 = f32[8,128,128]{2,1,0:T(8,128)S(1)} fusion(f32[8,128,128]{2,1,0:T(8,128)S(1)} %copy-done.3, f32[8,128,128]{2,1,0:T(8,128)S(1)} %bitcast.188, f32[4,128,128]{2,1,0:T(8,128)} %copy-done.31, f32[4,128,128]{2,1,0:T(8,128)} %copy-done.30, f32[16,136,136]{2,1,0:T(8,128)} %select_maximum_fusion.8, f32[8,128,128]{2,1,0:T(8,128)} %bitcast.194), kind=kLoop, calls=%fused_computation.252 | loop fusion | flops 6422528 | bytes 11010048 | tf_op jit(solution)/shard_map/add | solution.py:56
  222.1 6.3 %collective-permute-start.9 = (f32[4,128,128]{2,1,0:T(8,128)}, f32[4,128,128]{2,1,0:T(8,128)}, u32[]{:S(2)}, u32[]{:S(2)}) collective-permute-start(f32[4,128,128]{2,1,0:T(8,128)} %bitcast.33), channel_id=1, source_target_pairs={{0,1},{1,2},{2,3},{3,4},{4,5},{5,6},{6,7},{7,8},{8,9},{9,10},{10,1... | collective-permute-start | bytes 786440 | tf_op jit(solution)/shard_map/ppermute | solution.py:16
  231.9 3.8 scatter_fusion.1
  238.6 6.3 %collective-permute-start.5 = (f32[4,128,128]{2,1,0:T(8,128)}, f32[4,128,128]{2,1,0:T(8,128)}, u32[]{:S(2)}, u32[]{:S(2)}) collective-permute-start(f32[4,128,128]{2,1,0:T(8,128)} %get-tuple-element.60), channel_id=1, source_target_pairs={{0,1},{1,2},{2,3},{3,4},{4,5},{5,6},{6,7},{7,8},{8,9},{9,10},{10,1... | collective-permute-start | bytes 786440 | tf_op jit(solution)/shard_map/ppermute | solution.py:16
  246.7 3.5 fusion.98
  254.3 6.5 %collective-permute-start.11 = (f32[4,128,128]{2,1,0:T(8,128)S(1)}, f32[4,128,128]{2,1,0:T(8,128)S(1)}, u32[]{:S(2)}, u32[]{:S(2)}) collective-permute-start(f32[4,128,128]{2,1,0:T(8,128)S(1)} %bitcast.197), channel_id=1, source_target_pairs={{0,1},{1,2},{2,3},{3,4},{4,5},{5,6},{6,7},{7,8},{8,9},{9,10},{10,1... | collective-permute-start | bytes 786440 | tf_op jit(solution)/shard_map/ppermute | solution.py:16
  263.9 5.5 %collective-permute-done.11 = f32[4,128,128]{2,1,0:T(8,128)S(1)} collective-permute-done((f32[4,128,128]{2,1,0:T(8,128)S(1)}, f32[4,128,128]{2,1,0:T(8,128)S(1)}, u32[]{:S(2)}, u32[]{:S(2)}) %collective-permute-start.11) | collective-permute-done | bytes 262176 | tf_op jit(solution)/shard_map/ppermute | solution.py:16
  272.1 12.4 %fusion.72 = f32[8,128,128]{2,1,0:T(8,128)} fusion(f32[8,128,128]{2,1,0:T(8,128)S(1)} %copy-done.5, f32[8,128,128]{2,1,0:T(8,128)S(1)} %bitcast.177, f32[4,128,128]{2,1,0:T(8,128)} %copy-done.29, f32[4,128,128]{2,1,0:T(8,128)} %copy-done.28, f32[16,136,136]{2,1,0:T(8,128)} %select_maximum_fusion.4, f32[8,128,128]{2,1,0:T(8,128)S(1)} %bitcast.173), kind=kLoop, calls=%fused_computation.200 | loop fusion | flops 6422528 | bytes 11010048 | tf_op jit(solution)/shard_map/add | solution.py:56
  291.7 6.3 %collective-permute-start.13 = (f32[4,128,128]{2,1,0:T(8,128)}, f32[4,128,128]{2,1,0:T(8,128)}, u32[]{:S(2)}, u32[]{:S(2)}) collective-permute-start(f32[4,128,128]{2,1,0:T(8,128)} %bitcast.43), channel_id=1, source_target_pairs={{0,1},{1,2},{2,3},{3,4},{4,5},{5,6},{6,7},{7,8},{8,9},{9,10},{10,1... | collective-permute-start | bytes 786440 | tf_op jit(solution)/shard_map/ppermute | solution.py:16
  298.0 4.8 fusion.149
  302.8 5.0 scatter_fusion.2
  310.1 5.1 fusion.46
  325.5 6.3 %collective-permute-start.15 = (f32[4,128,128]{2,1,0:T(8,128)S(1)}, f32[4,128,128]{2,1,0:T(8,128)}, u32[]{:S(2)}, u32[]{:S(2)}) collective-permute-start(f32[4,128,128]{2,1,0:T(8,128)S(1)} %get-tuple-element.56), channel_id=1, source_target_pairs={{0,1},{1,2},{2,3},{3,4},{4,5},{5,6},{6,7},{7,8},{8,9},{9,10},{10,1... | collective-permute-start | bytes 786440 | tf_op jit(solution)/shard_map/ppermute | solution.py:16
  331.9 5.5 %gather_fusion.1 = f32[2048,128]{1,0:T(8,128)S(1)} fusion(f32[1024,128]{1,0:T(8,128)S(1)} %fusion.293, s32[2048]{0:T(1024)S(1)} %broadcast_clamp_fusion), kind=kCustom, calls=%fused_computation.1 | custom fusion | bytes 2105344 | tf_op jit(solution)/shard_map/gather | solution.py:150
  339.8 115.9 %all-reduce.11.cloned.1.call-done = f32[128,128]{1,0:T(8,128)} async-done(((f32[128,128]{1,0:T(8,128)}), f32[128,128]{1,0:T(8,128)}) %all-reduce.11.cloned.1.call-update) | async-done | bytes 65552
  458.7 4.9 fusion.20
  463.6 4.9 scatter_fusion.4
  470.5 50.8 %reduce-scatter.2.cloned.1.call-done = f32[8,8,128]{2,1,0:T(8,128)} async-done(((f32[8,128,128]{2,1,0:T(8,128)}), f32[8,8,128]{2,1,0:T(8,128)}) %reduce-scatter.2.cloned.1.call-update) | async-done | bytes 32784 | tf_op jit(solution)/shard_map/reduce_scatter | solution.py:151
  (159 shorter events, 79.2 us)
Async XLA Ops:
  32.9 142.2 %all-to-all-start = ((f32[2,16,32,8,128]{4,3,2,0,1:T(8,128)}), f32[2,16,32,8,128]{4,3,2,0,1:T(8,128)}, u32[]{:S(2)}, u32[]{:S(2)}) async-start(f32[2,16,32,8,128]{4,3,2,0,1:T(8,128)} %copy.35), calls=%async_computation | async-start | bytes 8388608 | tf_op jit(solution)/shard_map/all_to_all | solution.py:103
  44.4 17.8 %copy-start.36 = (s32[1,512]{1,0:T(1,128)S(1)}, s32[1,512]{1,0:T(1,128)}, u32[]{:S(2)}) copy-start(s32[1,512]{1,0:T(1,128)} %param.23) | copy-start | bytes 6148
  44.4 17.8 %copy-start.33 = (f32[1,4,512]{2,1,0:T(4,128)S(1)}, f32[1,4,512]{2,1,0:T(4,128)}, u32[]{:S(2)}) copy-start(f32[1,4,512]{2,1,0:T(4,128)} %param.24) | copy-start | bytes 24580
  44.5 18.4 %copy-start.35 = (f32[1,4]{1,0:T(1,128)S(1)}, f32[1,4]{1,0:T(1,128)}, u32[]{:S(2)}) copy-start(f32[1,4]{1,0:T(1,128)} %param.21) | copy-start | bytes 52
  44.5 19.0 %copy-start.34 = (s32[1,128,16]{1,2,0:T(8,128)S(1)}, s32[1,128,16]{1,2,0:T(8,128)}, u32[]{:S(2)}) copy-start(s32[1,128,16]{1,2,0:T(8,128)} %param.25) | copy-start | bytes 24580
  44.5 411.2 %all-reduce.11.cloned.1.call-start = ((), (), s32[]{:S(2)}) async-start(), calls=%async_computation.3 | async-start | bytes 131072
  44.6 101.4 %copy-start.22 = (f32[8,128,128]{2,1,0:T(8,128)}, f32[8,128,128]{2,1,0:T(8,128)S(1)}, u32[]{:S(2)}) copy-start(f32[8,128,128]{2,1,0:T(8,128)S(1)} %bitcast_multiply_fusion.5) | copy-start | bytes 1572868
  44.7 101.4 %collective-permute-start = (f32[4,128,128]{2,1,0:T(8,128)S(1)}, f32[4,128,128]{2,1,0:T(8,128)S(1)}, u32[]{:S(2)}, u32[]{:S(2)}) collective-permute-start(f32[4,128,128]{2,1,0:T(8,128)S(1)} %get-tuple-element.63), channel_id=1, source_target_pairs={{1,0},{2,1},{3,2},{4,3},{5,4},{6,5},{7,6},{8,7},{9,8},{10,9},{11,1... | collective-permute-start | bytes 786440 | tf_op jit(solution)/shard_map/ppermute | solution.py:17
  46.7 99.3 %collective-permute-start.1 = (f32[4,128,128]{2,1,0:T(8,128)S(1)}, f32[4,128,128]{2,1,0:T(8,128)S(1)}, u32[]{:S(2)}, u32[]{:S(2)}) collective-permute-start(f32[4,128,128]{2,1,0:T(8,128)S(1)} %get-tuple-element.64), channel_id=1, source_target_pairs={{0,1},{1,2},{2,3},{3,4},{4,5},{5,6},{6,7},{7,8},{8,9},{9,10},{10,1... | collective-permute-start | bytes 786440 | tf_op jit(solution)/shard_map/ppermute | solution.py:16
  155.9 11.9 %copy-start.19 = (f32[8,128,128]{2,1,0:T(8,128)}, f32[8,128,128]{2,1,0:T(8,128)S(1)}, u32[]{:S(2)}) copy-start(f32[8,128,128]{2,1,0:T(8,128)S(1)} %mul.453) | copy-start | bytes 1572868
  155.9 11.8 %collective-permute-start.2 = (f32[4,128,128]{2,1,0:T(8,128)S(1)}, f32[4,128,128]{2,1,0:T(8,128)S(1)}, u32[]{:S(2)}, u32[]{:S(2)}) collective-permute-start(f32[4,128,128]{2,1,0:T(8,128)S(1)} %get-tuple-element.61), channel_id=1, source_target_pairs={{1,0},{2,1},{3,2},{4,3},{5,4},{6,5},{7,6},{8,7},{9,8},{10,9},{11,1... | collective-permute-start | bytes 786440 | tf_op jit(solution)/shard_map/ppermute | solution.py:17
  158.0 15.4 %collective-permute-start.3 = (f32[4,128,128]{2,1,0:T(8,128)S(1)}, f32[4,128,128]{2,1,0:T(8,128)}, u32[]{:S(2)}, u32[]{:S(2)}) collective-permute-start(f32[4,128,128]{2,1,0:T(8,128)S(1)} %get-tuple-element.62), channel_id=1, source_target_pairs={{0,1},{1,2},{2,3},{3,4},{4,5},{5,6},{6,7},{7,8},{8,9},{9,10},{10,1... | collective-permute-start | bytes 786440 | tf_op jit(solution)/shard_map/ppermute | solution.py:16
  185.2 12.6 %collective-permute-start.6 = (f32[4,128,128]{2,1,0:T(8,128)S(1)}, f32[4,128,128]{2,1,0:T(8,128)S(1)}, u32[]{:S(2)}, u32[]{:S(2)}) collective-permute-start(f32[4,128,128]{2,1,0:T(8,128)S(1)} %bitcast.200), channel_id=1, source_target_pairs={{1,0},{2,1},{3,2},{4,3},{5,4},{6,5},{7,6},{8,7},{9,8},{10,9},{11,1... | collective-permute-start | bytes 786440 | tf_op jit(solution)/shard_map/ppermute | solution.py:17
  187.2 18.3 %copy-start.3 = (f32[8,128,128]{2,1,0:T(8,128)S(1)}, f32[8,128,128]{2,1,0:T(8,128)}, u32[]{:S(2)}) copy-start(f32[8,128,128]{2,1,0:T(8,128)} %param.17) | copy-start | bytes 1572868
  187.2 16.2 %collective-permute-start.7 = (f32[4,128,128]{2,1,0:T(8,128)S(1)}, f32[4,128,128]{2,1,0:T(8,128)S(1)}, u32[]{:S(2)}, u32[]{:S(2)}) collective-permute-start(f32[4,128,128]{2,1,0:T(8,128)S(1)} %bitcast.199), channel_id=1, source_target_pairs={{0,1},{1,2},{2,3},{3,4},{4,5},{5,6},{6,7},{7,8},{8,9},{9,10},{10,1... | collective-permute-start | bytes 786440 | tf_op jit(solution)/shard_map/ppermute | solution.py:16
  194.7 22.5 %copy-start.13 = (f32[1,128,8,128]{3,2,0,1:T(8,128)}, f32[1,128,8,128]{3,2,0,1:T(8,128)S(1)}, u32[]{:S(2)}) copy-start(f32[1,128,8,128]{3,2,0,1:T(8,128)S(1)} %get-tuple-element.52) | copy-start | bytes 1572868
  205.4 23.0 %copy-start.20 = (f32[8,128,128]{2,1,0:T(8,128)S(1)}, f32[8,128,128]{2,1,0:T(8,128)}, u32[]{:S(2)}) copy-start(f32[8,128,128]{2,1,0:T(8,128)} %copy-done.19) | copy-start | bytes 1572868
  219.3 12.6 %copy-start.7 = (f32[131072]{0:T(1024)}, f32[131072]{0:T(1024)S(1)}, u32[]{:S(2)}) copy-start(f32[131072]{0:T(1024)S(1)} %fusion.306) | copy-start | bytes 1572868
  220.2 24.7 %collective-permute-start.8 = (f32[4,128,128]{2,1,0:T(8,128)}, f32[4,128,128]{2,1,0:T(8,128)}, u32[]{:S(2)}, u32[]{:S(2)}) collective-permute-start(f32[4,128,128]{2,1,0:T(8,128)} %bitcast.32), channel_id=1, source_target_pairs={{1,0},{2,1},{3,2},{4,3},{5,4},{6,5},{7,6},{8,7},{9,8},{10,9},{11,1... | collective-permute-start | bytes 786440 | tf_op jit(solution)/shard_map/ppermute | solution.py:17
  222.1 22.8 %collective-permute-start.9 = (f32[4,128,128]{2,1,0:T(8,128)}, f32[4,128,128]{2,1,0:T(8,128)}, u32[]{:S(2)}, u32[]{:S(2)}) collective-permute-start(f32[4,128,128]{2,1,0:T(8,128)} %bitcast.33), channel_id=1, source_target_pairs={{0,1},{1,2},{2,3},{3,4},{4,5},{5,6},{6,7},{7,8},{8,9},{9,10},{10,1... | collective-permute-start | bytes 786440 | tf_op jit(solution)/shard_map/ppermute | solution.py:16
  236.7 24.2 %collective-permute-start.4 = (f32[4,128,128]{2,1,0:T(8,128)}, f32[4,128,128]{2,1,0:T(8,128)S(1)}, u32[]{:S(2)}, u32[]{:S(2)}) collective-permute-start(f32[4,128,128]{2,1,0:T(8,128)} %get-tuple-element.59), channel_id=1, source_target_pairs={{1,0},{2,1},{3,2},{4,3},{5,4},{6,5},{7,6},{8,7},{9,8},{10,9},{11,1... | collective-permute-start | bytes 786440 | tf_op jit(solution)/shard_map/ppermute | solution.py:17
  238.6 22.3 %collective-permute-start.5 = (f32[4,128,128]{2,1,0:T(8,128)}, f32[4,128,128]{2,1,0:T(8,128)}, u32[]{:S(2)}, u32[]{:S(2)}) collective-permute-start(f32[4,128,128]{2,1,0:T(8,128)} %get-tuple-element.60), channel_id=1, source_target_pairs={{0,1},{1,2},{2,3},{3,4},{4,5},{5,6},{6,7},{7,8},{8,9},{9,10},{10,1... | collective-permute-start | bytes 786440 | tf_op jit(solution)/shard_map/ppermute | solution.py:16
  252.3 19.8 %copy-start.10 = (f32[131072]{0:T(1024)}, f32[131072]{0:T(1024)S(1)}, u32[]{:S(2)}) copy-start(f32[131072]{0:T(1024)S(1)} %fusion.307) | copy-start | bytes 1572868
  252.4 11.5 %collective-permute-start.10 = (f32[4,128,128]{2,1,0:T(8,128)S(1)}, f32[4,128,128]{2,1,0:T(8,128)S(1)}, u32[]{:S(2)}, u32[]{:S(2)}) collective-permute-start(f32[4,128,128]{2,1,0:T(8,128)S(1)} %bitcast.198), channel_id=1, source_target_pairs={{1,0},{2,1},{3,2},{4,3},{5,4},{6,5},{7,6},{8,7},{9,8},{10,9},{11,1... | collective-permute-start | bytes 786440 | tf_op jit(solution)/shard_map/ppermute | solution.py:17
  254.3 15.1 %collective-permute-start.11 = (f32[4,128,128]{2,1,0:T(8,128)S(1)}, f32[4,128,128]{2,1,0:T(8,128)S(1)}, u32[]{:S(2)}, u32[]{:S(2)}) collective-permute-start(f32[4,128,128]{2,1,0:T(8,128)S(1)} %bitcast.197), channel_id=1, source_target_pairs={{0,1},{1,2},{2,3},{3,4},{4,5},{5,6},{6,7},{7,8},{8,9},{9,10},{10,1... | collective-permute-start | bytes 786440 | tf_op jit(solution)/shard_map/ppermute | solution.py:16
  289.8 18.0 %collective-permute-start.12 = (f32[4,128,128]{2,1,0:T(8,128)}, f32[4,128,128]{2,1,0:T(8,128)}, u32[]{:S(2)}, u32[]{:S(2)}) collective-permute-start(f32[4,128,128]{2,1,0:T(8,128)} %bitcast.42), channel_id=1, source_target_pairs={{1,0},{2,1},{3,2},{4,3},{5,4},{6,5},{7,6},{8,7},{9,8},{10,9},{11,1... | collective-permute-start | bytes 786440 | tf_op jit(solution)/shard_map/ppermute | solution.py:17
  291.7 16.5 %collective-permute-start.13 = (f32[4,128,128]{2,1,0:T(8,128)}, f32[4,128,128]{2,1,0:T(8,128)}, u32[]{:S(2)}, u32[]{:S(2)}) collective-permute-start(f32[4,128,128]{2,1,0:T(8,128)} %bitcast.43), channel_id=1, source_target_pairs={{0,1},{1,2},{2,3},{3,4},{4,5},{5,6},{6,7},{7,8},{8,9},{9,10},{10,1... | collective-permute-start | bytes 786440 | tf_op jit(solution)/shard_map/ppermute | solution.py:16
  323.6 133.3 %collective-permute-start.14 = (f32[4,128,128]{2,1,0:T(8,128)S(1)}, f32[4,128,128]{2,1,0:T(8,128)S(1)}, u32[]{:S(2)}, u32[]{:S(2)}) collective-permute-start(f32[4,128,128]{2,1,0:T(8,128)S(1)} %get-tuple-element.55), channel_id=1, source_target_pairs={{1,0},{2,1},{3,2},{4,3},{5,4},{6,5},{7,6},{8,7},{9,8},{10,9},{11,1... | collective-permute-start | bytes 786440 | tf_op jit(solution)/shard_map/ppermute | solution.py:17
  325.5 13.0 %copy-start.39 = (u32[256]{0:T(256)S(1)}, u32[256]{0:T(256)}, u32[]{:S(2)}) copy-start(u32[256]{0:T(256)} %constant.194) | copy-start | bytes 3076
  325.5 131.4 %collective-permute-start.15 = (f32[4,128,128]{2,1,0:T(8,128)S(1)}, f32[4,128,128]{2,1,0:T(8,128)}, u32[]{:S(2)}, u32[]{:S(2)}) collective-permute-start(f32[4,128,128]{2,1,0:T(8,128)S(1)} %get-tuple-element.56), channel_id=1, source_target_pairs={{0,1},{1,2},{2,3},{3,4},{4,5},{5,6},{6,7},{7,8},{8,9},{9,10},{10,1... | collective-permute-start | bytes 786440 | tf_op jit(solution)/shard_map/ppermute | solution.py:16
  338.1 120.6 %copy-start.1 = (f32[131072]{0:T(1024)S(1)}, f32[131072]{0:T(1024)}, u32[]{:S(2)}) copy-start(f32[131072]{0:T(1024)} %scatter_fusion.2) | copy-start | bytes 1572868
  338.2 183.1 %reduce-scatter.2.cloned.1.call-start = ((), (), s32[]{:S(2)}) async-start(), calls=%async_computation.2 | async-start | bytes 557056 | tf_op jit(solution)/shard_map/reduce_scatter | solution.py:151
  (27 other events, 153.7 us)
Sparse Core Ops, SparseCore 0:
  338.3 117.3 all-reduce.10
  458.8 62.5 reduce-scatter.1
where the time goes:
time: 530 us; the launch traced here: 528 us
  waiting for transfers between devices  271 us (51%)
  other arithmetic  105 us (20%)
  starting transfers between devices  78.5 us (15%)
  local copies, waits for them, and re-layouts  56.5 us (11%)
  between operations  16.6 us (3%)
    unnamed x3, waiting for transfers between devices  116 us
    ppermute x8, waiting for transfers between devices, padded_2(): after = lax.ppermute(initial, axis, down)  87.5 us
    ppermute x8, starting transfers between devices, padded_2(): before = lax.ppermute(last, axis, up)  51 us
    reduce_scatter x1, waiting for transfers between devices, body(): lax.psum_scatter(partial_value, 'shot', scatter_dimension=1, tiled=True)  50.8 us
    add x4, other arithmetic, advance(): 2.0 * current_ext[4:-4] - before + courant * laplace(current_ext)  32.8 us
    scatter-add x8, other arithmetic, inject(): flattened = field.reshape(-1).at[target].add(values, mode='drop')  28.2 us
    ppermute x8, waiting for transfers between devices, padded_2(): before = lax.ppermute(last, axis, up)  17.1 us
    add x4, other arithmetic, retreat(): earlier = 2.0 * current - following + laplace(weighted_ext)  16.5 us
  transfers between devices with their start and end apart: 19, of which 10 were waited for; matrix products, arithmetic and copies ran while one was open for 14% of the time, Pallas kernels for 0%

commit v1 on v0

--- a/solution.py
+++ b/solution.py
@@ -100,7 +100,12 @@
         .set(payload)
     )
     outgoing = outgoing.reshape(2, devices, capacity, block_rows, breadth)
-    incoming = lax.all_to_all(outgoing, "space", split_axis=1, concat_axis=1, tiled=True)
+    incoming = jnp.concatenate(
+        lax.all_to_all(
+            jnp.stack(jnp.split(outgoing, lax.axis_size("space"), axis=1)), "space", 0, 0
+        ),
+        axis=1,
+    )
     incoming = incoming.reshape(2, devices * capacity, block_rows, breadth)
     sender_grid = jnp.arange(devices, dtype=jnp.int32)[:, None] * capacity + ranking
     owned = peer_grid == position

time: 530 us -> 545 us (1.028)
  local copies, waits for them, and re-layouts: 56.5 us -> 71.1 us
    unnamed x81 -> x98, local copies, waits for them, and re-layouts: 3.47 us -> 22.1 us
  transfers between devices with their start and end apart: 19 -> 19, of which waited for: 10 -> 9; matrix products, arithmetic and copies ran while one was open for 14% -> 13% of each run, Pallas kernels for 0% -> 0%
where the time goes in v1:
time: 545 us; the launch traced here: 543 us
  waiting for transfers between devices  271 us (50%)
  other arithmetic  106 us (19%)
  starting transfers between devices  78.5 us (14%)
  local copies, waits for them, and re-layouts  71.1 us (13%)
  between operations  16.7 us (3%)
    unnamed x3, waiting for transfers between devices  116 us
    ppermute x8, waiting for transfers between devices, padded_2(): after = lax.ppermute(initial, axis, down)  87.3 us
    ppermute x8, starting transfers between devices, padded_2(): before = lax.ppermute(last, axis, up)  51 us
    reduce_scatter x1, waiting for transfers between devices, body(): lax.psum_scatter(partial_value, 'shot', scatter_dimension=1, tiled=True)  50.9 us
    add x4, other arithmetic, advance(): 2.0 * current_ext[4:-4] - before + courant * laplace(current_ext)  33 us
    scatter-add x8, other arithmetic, inject(): flattened = field.reshape(-1).at[target].add(values, mode='drop')  28.2 us
    unnamed x98, local copies, waits for them, and re-layouts  22.1 us
    add x4, other arithmetic, retreat(): earlier = 2.0 * current - following + laplace(weighted_ext)  16.9 us
  transfers between devices with their start and end apart: 19, of which 9 were waited for; matrix products, arithmetic and copies ran while one was open for 13% of the time, Pallas kernels for 0%

profile of v1, /device:TPU:4, one launch (start us, length us, event | category | flops | bytes accessed | tf_op | source)
XLA Modules:
  0.0 543.2 jit_solution(3577778192889454916)
XLA Ops:
  14.6 13.6 %scatter_fusion.3 = f32[2,512,8,128]{3,2,1,0:T(8,128)} fusion(f32[2,512,8,128]{3,2,1,0:T(8,128)} %broadcast_in_dim.48, s32[128]{0:T(128)S(1)} %fusion.326, f32[128,2,8,128]{3,2,1,0:T(8,128)S(1)} %copy.95), kind=kCustom, calls=%fused_computation.6 | custom fusion | bytes 3146240 | tf_op jit(solution)/shard_map/scatter | solution.py:100
  47.5 11.6 %all-to-all-start = ((f32[16,2,1,32,8,128]{5,4,3,1,2,0:T(8,128)}), f32[16,2,1,32,8,128]{5,4,3,1,2,0:T(8,128)}, u32[]{:S(2)}, u32[]{:S(2)}) async-start(f32[16,2,1,32,8,128]{5,4,3,1,2,0:T(8,128)} %fusion.304), calls=%async_computation | async-start | bytes 8388608 | tf_op jit(solution)/shard_map/all_to_all | solution.py:104
  61.4 6.2 %collective-permute-start.1 = (f32[4,128,128]{2,1,0:T(8,128)S(1)}, f32[4,128,128]{2,1,0:T(8,128)S(1)}, u32[]{:S(2)}, u32[]{:S(2)}) collective-permute-start(f32[4,128,128]{2,1,0:T(8,128)S(1)} %get-tuple-element.64), channel_id=1, source_target_pairs={{0,1},{1,2},{2,3},{3,4},{4,5},{5,6},{6,7},{7,8},{8,9},{9,10},{10,1... | collective-permute-start | bytes 786440 | tf_op jit(solution)/shard_map/ppermute | solution.py:16
  67.8 8.0 %scatter_custom_fusion.3 = s32[128]{0:T(128)S(1)} fusion(s32[2048]{0:T(1024)S(1)} %bitcast.323, s32[2048]{0:T(1024)S(1)} %add_bitcast_fusion, s32[]{:T(128)} %constant.152.clone.1), kind=kCustom, calls=%fused_computation.596 | custom fusion | bytes 516 | tf_op jit(solution)/shard_map/scatter | solution.py:116
  78.3 82.4 %collective-permute-done = f32[4,128,128]{2,1,0:T(8,128)S(1)} collective-permute-done((f32[4,128,128]{2,1,0:T(8,128)S(1)}, f32[4,128,128]{2,1,0:T(8,128)S(1)}, u32[]{:S(2)}, u32[]{:S(2)}) %collective-permute-start) | collective-permute-done | bytes 262176 | tf_op jit(solution)/shard_map/ppermute | solution.py:17
  163.2 3.5 fusion.199
  166.7 3.7 scatter_fusion
  172.6 6.3 %collective-permute-start.3 = (f32[4,128,128]{2,1,0:T(8,128)S(1)}, f32[4,128,128]{2,1,0:T(8,128)}, u32[]{:S(2)}, u32[]{:S(2)}) collective-permute-start(f32[4,128,128]{2,1,0:T(8,128)S(1)} %get-tuple-element.62), channel_id=1, source_target_pairs={{0,1},{1,2},{2,3},{3,4},{4,5},{5,6},{6,7},{7,8},{8,9},{9,10},{10,1... | collective-permute-start | bytes 786440 | tf_op jit(solution)/shard_map/ppermute | solution.py:16
  182.4 5.6 %collective-permute-done.3 = f32[4,128,128]{2,1,0:T(8,128)} collective-permute-done((f32[4,128,128]{2,1,0:T(8,128)S(1)}, f32[4,128,128]{2,1,0:T(8,128)}, u32[]{:S(2)}, u32[]{:S(2)}) %collective-permute-start.3) | collective-permute-done | bytes 262176 | tf_op jit(solution)/shard_map/ppermute | solution.py:16
  189.8 4.7 copy.112
  194.4 4.0 gather_fusion
  201.8 6.6 %collective-permute-start.7 = (f32[4,128,128]{2,1,0:T(8,128)S(1)}, f32[4,128,128]{2,1,0:T(8,128)S(1)}, u32[]{:S(2)}, u32[]{:S(2)}) collective-permute-start(f32[4,128,128]{2,1,0:T(8,128)S(1)} %bitcast.312), channel_id=1, source_target_pairs={{0,1},{1,2},{2,3},{3,4},{4,5},{5,6},{6,7},{7,8},{8,9},{9,10},{10,1... | collective-permute-start | bytes 786440 | tf_op jit(solution)/shard_map/ppermute | solution.py:16
  212.5 5.5 %collective-permute-done.7 = f32[4,128,128]{2,1,0:T(8,128)S(1)} collective-permute-done((f32[4,128,128]{2,1,0:T(8,128)S(1)}, f32[4,128,128]{2,1,0:T(8,128)S(1)}, u32[]{:S(2)}, u32[]{:S(2)}) %collective-permute-start.7) | collective-permute-done | bytes 262176 | tf_op jit(solution)/shard_map/ppermute | solution.py:16
  220.1 11.8 %fusion.124 = f32[8,128,128]{2,1,0:T(8,128)S(1)} fusion(f32[8,128,128]{2,1,0:T(8,128)S(1)} %copy-done.3, f32[8,128,128]{2,1,0:T(8,128)S(1)} %bitcast.301, f32[4,128,128]{2,1,0:T(8,128)} %copy-done.32, f32[4,128,128]{2,1,0:T(8,128)} %copy-done.31, f32[16,136,136]{2,1,0:T(8,128)} %select_maximum_fusion.8, f32[8,128,128]{2,1,0:T(8,128)} %bitcast.307), kind=kLoop, calls=%fused_computation.252 | loop fusion | flops 6422528 | bytes 11010048 | tf_op jit(solution)/shard_map/add | solution.py:56
  236.7 6.3 %collective-permute-start.9 = (f32[4,128,128]{2,1,0:T(8,128)}, f32[4,128,128]{2,1,0:T(8,128)}, u32[]{:S(2)}, u32[]{:S(2)}) collective-permute-start(f32[4,128,128]{2,1,0:T(8,128)} %bitcast.50), channel_id=1, source_target_pairs={{0,1},{1,2},{2,3},{3,4},{4,5},{5,6},{6,7},{7,8},{8,9},{9,10},{10,1... | collective-permute-start | bytes 786440 | tf_op jit(solution)/shard_map/ppermute | solution.py:16
  246.5 3.8 scatter_fusion.1
  253.2 6.3 %collective-permute-start.5 = (f32[4,128,128]{2,1,0:T(8,128)}, f32[4,128,128]{2,1,0:T(8,128)}, u32[]{:S(2)}, u32[]{:S(2)}) collective-permute-start(f32[4,128,128]{2,1,0:T(8,128)} %get-tuple-element.60), channel_id=1, source_target_pairs={{0,1},{1,2},{2,3},{3,4},{4,5},{5,6},{6,7},{7,8},{8,9},{9,10},{10,1... | collective-permute-start | bytes 786440 | tf_op jit(solution)/shard_map/ppermute | solution.py:16
  261.2 3.5 fusion.98
  268.9 6.5 %collective-permute-start.11 = (f32[4,128,128]{2,1,0:T(8,128)S(1)}, f32[4,128,128]{2,1,0:T(8,128)S(1)}, u32[]{:S(2)}, u32[]{:S(2)}) collective-permute-start(f32[4,128,128]{2,1,0:T(8,128)S(1)} %bitcast.310), channel_id=1, source_target_pairs={{0,1},{1,2},{2,3},{3,4},{4,5},{5,6},{6,7},{7,8},{8,9},{9,10},{10,1... | collective-permute-start | bytes 786440 | tf_op jit(solution)/shard_map/ppermute | solution.py:16
  278.4 5.5 %collective-permute-done.11 = f32[4,128,128]{2,1,0:T(8,128)S(1)} collective-permute-done((f32[4,128,128]{2,1,0:T(8,128)S(1)}, f32[4,128,128]{2,1,0:T(8,128)S(1)}, u32[]{:S(2)}, u32[]{:S(2)}) %collective-permute-start.11) | collective-permute-done | bytes 262176 | tf_op jit(solution)/shard_map/ppermute | solution.py:16
  286.7 12.5 %fusion.72 = f32[8,128,128]{2,1,0:T(8,128)} fusion(f32[8,128,128]{2,1,0:T(8,128)S(1)} %copy-done.5, f32[8,128,128]{2,1,0:T(8,128)S(1)} %bitcast.275, f32[4,128,128]{2,1,0:T(8,128)} %copy-done.30, f32[4,128,128]{2,1,0:T(8,128)} %copy-done.29, f32[16,136,136]{2,1,0:T(8,128)} %select_maximum_fusion.4, f32[8,128,128]{2,1,0:T(8,128)S(1)} %bitcast.271), kind=kLoop, calls=%fused_computation.200 | loop fusion | flops 6422528 | bytes 11010048 | tf_op jit(solution)/shard_map/add | solution.py:56
  299.2 3.4 fusion.324
  306.4 6.3 %collective-permute-start.13 = (f32[4,128,128]{2,1,0:T(8,128)}, f32[4,128,128]{2,1,0:T(8,128)}, u32[]{:S(2)}, u32[]{:S(2)}) collective-permute-start(f32[4,128,128]{2,1,0:T(8,128)} %bitcast.60), channel_id=1, source_target_pairs={{0,1},{1,2},{2,3},{3,4},{4,5},{5,6},{6,7},{7,8},{8,9},{9,10},{10,1... | collective-permute-start | bytes 786440 | tf_op jit(solution)/shard_map/ppermute | solution.py:16
  312.8 5.2 fusion.149
  317.9 5.0 scatter_fusion.2
  324.9 5.0 fusion.46
  340.4 6.3 %collective-permute-start.15 = (f32[4,128,128]{2,1,0:T(8,128)S(1)}, f32[4,128,128]{2,1,0:T(8,128)}, u32[]{:S(2)}, u32[]{:S(2)}) collective-permute-start(f32[4,128,128]{2,1,0:T(8,128)S(1)} %get-tuple-element.56), channel_id=1, source_target_pairs={{0,1},{1,2},{2,3},{3,4},{4,5},{5,6},{6,7},{7,8},{8,9},{9,10},{10,1... | collective-permute-start | bytes 786440 | tf_op jit(solution)/shard_map/ppermute | solution.py:16
  346.7 5.5 %gather_fusion.1 = f32[2048,128]{1,0:T(8,128)S(1)} fusion(f32[1024,128]{1,0:T(8,128)S(1)} %fusion.293, s32[2048]{0:T(1024)S(1)} %broadcast_clamp_fusion), kind=kCustom, calls=%fused_computation.1 | custom fusion | bytes 2105344 | tf_op jit(solution)/shard_map/gather | solution.py:155
  354.6 116.2 %all-reduce.11.cloned.1.call-done = f32[128,128]{1,0:T(8,128)} async-done(((f32[128,128]{1,0:T(8,128)}), f32[128,128]{1,0:T(8,128)}) %all-reduce.11.cloned.1.call-update) | async-done | bytes 65552
  473.8 4.8 fusion.20
  478.6 4.8 scatter_fusion.4
  485.5 50.9 %reduce-scatter.2.cloned.1.call-done = f32[8,8,128]{2,1,0:T(8,128)} async-done(((f32[8,128,128]{2,1,0:T(8,128)}), f32[8,8,128]{2,1,0:T(8,128)}) %reduce-scatter.2.cloned.1.call-update) | async-done | bytes 32784 | tf_op jit(solution)/shard_map/reduce_scatter | solution.py:156
  (176 shorter events, 94.9 us)
Async XLA Ops:
  28.2 13.5 %copy-start.12 = (f32[2,512,8,128]{3,2,1,0:T(8,128)S(1)}, f32[2,512,8,128]{3,2,1,0:T(8,128)}, u32[]{:S(2)}) copy-start(f32[2,512,8,128]{3,2,1,0:T(8,128)} %scatter_fusion.3) | copy-start | bytes 12582916
  47.5 142.3 %all-to-all-start = ((f32[16,2,1,32,8,128]{5,4,3,1,2,0:T(8,128)}), f32[16,2,1,32,8,128]{5,4,3,1,2,0:T(8,128)}, u32[]{:S(2)}, u32[]{:S(2)}) async-start(f32[16,2,1,32,8,128]{5,4,3,1,2,0:T(8,128)} %fusion.304), calls=%async_computation | async-start | bytes 8388608 | tf_op jit(solution)/shard_map/all_to_all | solution.py:104
  59.1 17.9 %copy-start.37 = (s32[1,512]{1,0:T(1,128)S(1)}, s32[1,512]{1,0:T(1,128)}, u32[]{:S(2)}) copy-start(s32[1,512]{1,0:T(1,128)} %param.23) | copy-start | bytes 6148
  59.1 17.9 %copy-start.34 = (f32[1,4,512]{2,1,0:T(4,128)S(1)}, f32[1,4,512]{2,1,0:T(4,128)}, u32[]{:S(2)}) copy-start(f32[1,4,512]{2,1,0:T(4,128)} %param.24) | copy-start | bytes 24580
  59.1 18.5 %copy-start.36 = (f32[1,4]{1,0:T(1,128)S(1)}, f32[1,4]{1,0:T(1,128)}, u32[]{:S(2)}) copy-start(f32[1,4]{1,0:T(1,128)} %param.21) | copy-start | bytes 52
  59.1 19.2 %copy-start.35 = (s32[1,128,16]{1,2,0:T(8,128)S(1)}, s32[1,128,16]{1,2,0:T(8,128)}, u32[]{:S(2)}) copy-start(s32[1,128,16]{1,2,0:T(8,128)} %param.25) | copy-start | bytes 24580
  59.1 411.6 %all-reduce.11.cloned.1.call-start = ((), (), s32[]{:S(2)}) async-start(), calls=%async_computation.3 | async-start | bytes 131072
  59.3 101.4 %copy-start.23 = (f32[8,128,128]{2,1,0:T(8,128)}, f32[8,128,128]{2,1,0:T(8,128)S(1)}, u32[]{:S(2)}) copy-start(f32[8,128,128]{2,1,0:T(8,128)S(1)} %bitcast_multiply_fusion.5) | copy-start | bytes 1572868
  59.3 101.4 %collective-permute-start = (f32[4,128,128]{2,1,0:T(8,128)S(1)}, f32[4,128,128]{2,1,0:T(8,128)S(1)}, u32[]{:S(2)}, u32[]{:S(2)}) collective-permute-start(f32[4,128,128]{2,1,0:T(8,128)S(1)} %get-tuple-element.63), channel_id=1, source_target_pairs={{1,0},{2,1},{3,2},{4,3},{5,4},{6,5},{7,6},{8,7},{9,8},{10,9},{11,1... | collective-permute-start | bytes 786440 | tf_op jit(solution)/shard_map/ppermute | solution.py:17
  61.4 99.3 %collective-permute-start.1 = (f32[4,128,128]{2,1,0:T(8,128)S(1)}, f32[4,128,128]{2,1,0:T(8,128)S(1)}, u32[]{:S(2)}, u32[]{:S(2)}) collective-permute-start(f32[4,128,128]{2,1,0:T(8,128)S(1)} %get-tuple-element.64), channel_id=1, source_target_pairs={{0,1},{1,2},{2,3},{3,4},{4,5},{5,6},{6,7},{7,8},{8,9},{9,10},{10,1... | collective-permute-start | bytes 786440 | tf_op jit(solution)/shard_map/ppermute | solution.py:16
  170.6 11.8 %collective-permute-start.2 = (f32[4,128,128]{2,1,0:T(8,128)S(1)}, f32[4,128,128]{2,1,0:T(8,128)S(1)}, u32[]{:S(2)}, u32[]{:S(2)}) collective-permute-start(f32[4,128,128]{2,1,0:T(8,128)S(1)} %get-tuple-element.61), channel_id=1, source_target_pairs={{1,0},{2,1},{3,2},{4,3},{5,4},{6,5},{7,6},{8,7},{9,8},{10,9},{11,1... | collective-permute-start | bytes 786440 | tf_op jit(solution)/shard_map/ppermute | solution.py:17
  172.6 15.4 %collective-permute-start.3 = (f32[4,128,128]{2,1,0:T(8,128)S(1)}, f32[4,128,128]{2,1,0:T(8,128)}, u32[]{:S(2)}, u32[]{:S(2)}) collective-permute-start(f32[4,128,128]{2,1,0:T(8,128)S(1)} %get-tuple-element.62), channel_id=1, source_target_pairs={{0,1},{1,2},{2,3},{3,4},{4,5},{5,6},{6,7},{7,8},{8,9},{9,10},{10,1... | collective-permute-start | bytes 786440 | tf_op jit(solution)/shard_map/ppermute | solution.py:16
  199.9 12.6 %collective-permute-start.6 = (f32[4,128,128]{2,1,0:T(8,128)S(1)}, f32[4,128,128]{2,1,0:T(8,128)S(1)}, u32[]{:S(2)}, u32[]{:S(2)}) collective-permute-start(f32[4,128,128]{2,1,0:T(8,128)S(1)} %bitcast.313), channel_id=1, source_target_pairs={{1,0},{2,1},{3,2},{4,3},{5,4},{6,5},{7,6},{8,7},{9,8},{10,9},{11,1... | collective-permute-start | bytes 786440 | tf_op jit(solution)/shard_map/ppermute | solution.py:17
  201.8 18.2 %copy-start.3 = (f32[8,128,128]{2,1,0:T(8,128)S(1)}, f32[8,128,128]{2,1,0:T(8,128)}, u32[]{:S(2)}) copy-start(f32[8,128,128]{2,1,0:T(8,128)} %param.17) | copy-start | bytes 1572868
  201.8 16.2 %collective-permute-start.7 = (f32[4,128,128]{2,1,0:T(8,128)S(1)}, f32[4,128,128]{2,1,0:T(8,128)S(1)}, u32[]{:S(2)}, u32[]{:S(2)}) collective-permute-start(f32[4,128,128]{2,1,0:T(8,128)S(1)} %bitcast.312), channel_id=1, source_target_pairs={{0,1},{1,2},{2,3},{3,4},{4,5},{5,6},{6,7},{7,8},{8,9},{9,10},{10,1... | collective-permute-start | bytes 786440 | tf_op jit(solution)/shard_map/ppermute | solution.py:16
  209.4 22.6 %copy-start.14 = (f32[1,128,8,128]{3,2,0,1:T(8,128)}, f32[1,128,8,128]{3,2,0,1:T(8,128)S(1)}, u32[]{:S(2)}) copy-start(f32[1,128,8,128]{3,2,0,1:T(8,128)S(1)} %get-tuple-element.52) | copy-start | bytes 1572868
  220.1 23.0 %copy-start.21 = (f32[8,128,128]{2,1,0:T(8,128)S(1)}, f32[8,128,128]{2,1,0:T(8,128)}, u32[]{:S(2)}) copy-start(f32[8,128,128]{2,1,0:T(8,128)} %copy-done.20) | copy-start | bytes 1572868
  233.9 12.6 %copy-start.7 = (f32[131072]{0:T(1024)}, f32[131072]{0:T(1024)S(1)}, u32[]{:S(2)}) copy-start(f32[131072]{0:T(1024)S(1)} %fusion.322) | copy-start | bytes 1572868
  234.8 24.7 %collective-permute-start.8 = (f32[4,128,128]{2,1,0:T(8,128)}, f32[4,128,128]{2,1,0:T(8,128)}, u32[]{:S(2)}, u32[]{:S(2)}) collective-permute-start(f32[4,128,128]{2,1,0:T(8,128)} %bitcast.49), channel_id=1, source_target_pairs={{1,0},{2,1},{3,2},{4,3},{5,4},{6,5},{7,6},{8,7},{9,8},{10,9},{11,1... | collective-permute-start | bytes 786440 | tf_op jit(solution)/shard_map/ppermute | solution.py:17
  236.7 22.8 %collective-permute-start.9 = (f32[4,128,128]{2,1,0:T(8,128)}, f32[4,128,128]{2,1,0:T(8,128)}, u32[]{:S(2)}, u32[]{:S(2)}) collective-permute-start(f32[4,128,128]{2,1,0:T(8,128)} %bitcast.50), channel_id=1, source_target_pairs={{0,1},{1,2},{2,3},{3,4},{4,5},{5,6},{6,7},{7,8},{8,9},{9,10},{10,1... | collective-permute-start | bytes 786440 | tf_op jit(solution)/shard_map/ppermute | solution.py:16
  251.3 24.2 %collective-permute-start.4 = (f32[4,128,128]{2,1,0:T(8,128)}, f32[4,128,128]{2,1,0:T(8,128)S(1)}, u32[]{:S(2)}, u32[]{:S(2)}) collective-permute-start(f32[4,128,128]{2,1,0:T(8,128)} %get-tuple-element.59), channel_id=1, source_target_pairs={{1,0},{2,1},{3,2},{4,3},{5,4},{6,5},{7,6},{8,7},{9,8},{10,9},{11,1... | collective-permute-start | bytes 786440 | tf_op jit(solution)/shard_map/ppermute | solution.py:17
  253.2 22.3 %collective-permute-start.5 = (f32[4,128,128]{2,1,0:T(8,128)}, f32[4,128,128]{2,1,0:T(8,128)}, u32[]{:S(2)}, u32[]{:S(2)}) collective-permute-start(f32[4,128,128]{2,1,0:T(8,128)} %get-tuple-element.60), channel_id=1, source_target_pairs={{0,1},{1,2},{2,3},{3,4},{4,5},{5,6},{6,7},{7,8},{8,9},{9,10},{10,1... | collective-permute-start | bytes 786440 | tf_op jit(solution)/shard_map/ppermute | solution.py:16
  266.9 19.8 %copy-start.10 = (f32[131072]{0:T(1024)}, f32[131072]{0:T(1024)S(1)}, u32[]{:S(2)}) copy-start(f32[131072]{0:T(1024)S(1)} %fusion.323) | copy-start | bytes 1572868
  266.9 11.5 %collective-permute-start.10 = (f32[4,128,128]{2,1,0:T(8,128)S(1)}, f32[4,128,128]{2,1,0:T(8,128)S(1)}, u32[]{:S(2)}, u32[]{:S(2)}) collective-permute-start(f32[4,128,128]{2,1,0:T(8,128)S(1)} %bitcast.311), channel_id=1, source_target_pairs={{1,0},{2,1},{3,2},{4,3},{5,4},{6,5},{7,6},{8,7},{9,8},{10,9},{11,1... | collective-permute-start | bytes 786440 | tf_op jit(solution)/shard_map/ppermute | solution.py:17
  268.9 15.1 %collective-permute-start.11 = (f32[4,128,128]{2,1,0:T(8,128)S(1)}, f32[4,128,128]{2,1,0:T(8,128)S(1)}, u32[]{:S(2)}, u32[]{:S(2)}) collective-permute-start(f32[4,128,128]{2,1,0:T(8,128)S(1)} %bitcast.310), channel_id=1, source_target_pairs={{0,1},{1,2},{2,3},{3,4},{4,5},{5,6},{6,7},{7,8},{8,9},{9,10},{10,1... | collective-permute-start | bytes 786440 | tf_op jit(solution)/shard_map/ppermute | solution.py:16
  304.5 18.4 %collective-permute-start.12 = (f32[4,128,128]{2,1,0:T(8,128)}, f32[4,128,128]{2,1,0:T(8,128)}, u32[]{:S(2)}, u32[]{:S(2)}) collective-permute-start(f32[4,128,128]{2,1,0:T(8,128)} %bitcast.59), channel_id=1, source_target_pairs={{1,0},{2,1},{3,2},{4,3},{5,4},{6,5},{7,6},{8,7},{9,8},{10,9},{11,1... | collective-permute-start | bytes 786440 | tf_op jit(solution)/shard_map/ppermute | solution.py:17
  306.4 16.5 %collective-permute-start.13 = (f32[4,128,128]{2,1,0:T(8,128)}, f32[4,128,128]{2,1,0:T(8,128)}, u32[]{:S(2)}, u32[]{:S(2)}) collective-permute-start(f32[4,128,128]{2,1,0:T(8,128)} %bitcast.60), channel_id=1, source_target_pairs={{0,1},{1,2},{2,3},{3,4},{4,5},{5,6},{6,7},{7,8},{8,9},{9,10},{10,1... | collective-permute-start | bytes 786440 | tf_op jit(solution)/shard_map/ppermute | solution.py:16
  338.4 133.6 %collective-permute-start.14 = (f32[4,128,128]{2,1,0:T(8,128)S(1)}, f32[4,128,128]{2,1,0:T(8,128)S(1)}, u32[]{:S(2)}, u32[]{:S(2)}) collective-permute-start(f32[4,128,128]{2,1,0:T(8,128)S(1)} %get-tuple-element.55), channel_id=1, source_target_pairs={{1,0},{2,1},{3,2},{4,3},{5,4},{6,5},{7,6},{8,7},{9,8},{10,9},{11,1... | collective-permute-start | bytes 786440 | tf_op jit(solution)/shard_map/ppermute | solution.py:17
  340.3 12.9 %copy-start.40 = (u32[256]{0:T(256)S(1)}, u32[256]{0:T(256)}, u32[]{:S(2)}) copy-start(u32[256]{0:T(256)} %constant.194) | copy-start | bytes 3076
  340.4 131.7 %collective-permute-start.15 = (f32[4,128,128]{2,1,0:T(8,128)S(1)}, f32[4,128,128]{2,1,0:T(8,128)}, u32[]{:S(2)}, u32[]{:S(2)}) collective-permute-start(f32[4,128,128]{2,1,0:T(8,128)S(1)} %get-tuple-element.56), channel_id=1, source_target_pairs={{0,1},{1,2},{2,3},{3,4},{4,5},{5,6},{6,7},{7,8},{8,9},{9,10},{10,1... | collective-permute-start | bytes 786440 | tf_op jit(solution)/shard_map/ppermute | solution.py:16
  352.9 120.8 %copy-start.1 = (f32[131072]{0:T(1024)S(1)}, f32[131072]{0:T(1024)}, u32[]{:S(2)}) copy-start(f32[131072]{0:T(1024)} %scatter_fusion.2) | copy-start | bytes 1572868
  353.0 183.4 %reduce-scatter.2.cloned.1.call-start = ((), (), s32[]{:S(2)}) async-start(), calls=%async_computation.2 | async-start | bytes 557056 | tf_op jit(solution)/shard_map/reduce_scatter | solution.py:156
  (28 other events, 165.3 us)
Sparse Core Ops, SparseCore 0:
  353.1 117.6 all-reduce.10
  473.8 62.5 reduce-scatter.1
